TPU v7x, 512 devices: a whole 4x4x16 slice. The times are simulated.
512 devices in a mesh: dir: 8 (over z_lo), row: 64 (over x, y, z_hi, core).
Axes of the slice: x: 4, y: 4, z: 16 (z_hi: 2, z_lo: 8; z = z_hi * 8 + z_lo), core: 2. Of those that a mesh axis runs over, the one named last changes fastest.
Arguments:
- white_noise: bfloat16 [2, 8192, 8192], P(None, ('dir', 'row')), may hold values from -6 to 6
- geometry: int32 [8, 2], P('dir'), may hold values from 0 to 3
- window: int32 [8], P('dir'), may hold values from 1 to 8, as said below
- tile_map: int32 [8, 8192], P('dir'), may hold values from 0 to 65535
- link_gain: float32 [8, 8192], P('dir'), may hold values from 0.1 to 1
- serving: int32 [8192], replicated, may hold values from 0 to 7
Outputs:
- fluctuation: float32 [8, 512, 128], P('dir', 'row')
- signal_ratio: float32 [8192], P(('dir', 'row'))
Inputs may be any that keep to these rules, and one draw needn't show every extreme that they name: geometry[d,0] is direction d's Fresnel-scale bin and geometry[d,1] its slant bin. `window`: some direction has the half-width 8. `tile_map`: tile (t,u) is numbered t * 128 + u.
All inputs are finite; a program needn't handle non-finite values.
Results may differ from a plain program's by a relative error of at most 0.034.
Values may be sent and summed in bfloat16 or wider, within the bound.
No kernel may reach another device: no remote copies, remote signals or barrier semaphores. Data moves between devices by JAX's collectives and lax.ppermute only.
A program may use at most 64 MiB of HBM per device.

v0:
```python
import math
import jax
import jax.numpy as jnp
from jax import lax
from jax.sharding import PartitionSpec as P

N = 8192
FIRST = 64
SECOND = 128
ROWS_DEV = 32
XTILES = 128
YTILES = 8
TILE_X = 64
full_turn = 2.0 * math.pi
noise_floor = 0.05
tiny_value = 1e-06
strength = 1.6
row_patterns = (
    "zrab,zwak->wrkb",
    "zrkb,zwbc->wrkc",
    "zrkc,wzbc->wrkb",
    "zrkb,wzak->wrab",
    "zrkb,zak->rab",
)
column_patterns = (
    "zaby,zwak->wkby",
    "zkby,zwbc->wkcy",
    "zkcy,wzbc->wkby",
    "zkby,wzak->waby",
    "zkby,zak->aby",
)


def complex_block(real_part, imag_part):
    return jnp.stack(
        [jnp.stack([real_part, imag_part]), jnp.stack([-imag_part, real_part])]
    ).astype(jnp.bfloat16)


def transform_tables(first, second):
    total = first * second
    outer_ids = jnp.arange(first, dtype=jnp.int32)
    inner_ids = jnp.arange(second, dtype=jnp.int32)
    outer_angle = (outer_ids[:, None] * outer_ids[None, :] % first).astype(jnp.float32) * (
        full_turn / first
    )
    inner_angle = (inner_ids[:, None] * inner_ids[None, :] % second).astype(jnp.float32) * (
        full_turn / second
    )
    twist_angle = (outer_ids[:, None] * inner_ids[None, :] % total).astype(jnp.float32) * (
        full_turn / total
    )
    return (
        complex_block(jnp.cos(outer_angle), -jnp.sin(outer_angle)),
        complex_block(jnp.cos(inner_angle), -jnp.sin(inner_angle)),
        jnp.cos(twist_angle),
        -jnp.sin(twist_angle),
    )


def signed_wave(positions, first, second):
    total = first * second
    wave_number = positions // second + first * (positions % second)
    return jnp.where(wave_number >= total // 2, wave_number - total, wave_number).astype(
        jnp.float32
    )


def spectral_filter(row_ids, column_ids):
    wave_rows = signed_wave(row_ids, FIRST, SECOND)
    wave_columns = signed_wave(column_ids, FIRST, SECOND)
    squared_radius = 16.0 + wave_rows[:, None] ** 2 + wave_columns[None, :] ** 2
    return strength * float(N) * float(N) * squared_radius ** (-0.75)


def fresnel_factor(geometry_row, first, second):
    total = first * second
    fresnel_area = 144.0 * jnp.exp2(geometry_row[0].astype(jnp.float32))
    positions = jnp.arange(total, dtype=jnp.int32).reshape(first, second)
    scaled = signed_wave(positions, first, second) * (full_turn / total)
    turning = 0.5 * scaled * scaled * fresnel_area
    return (jnp.cos(turning), -jnp.sin(turning))


def complex_times(values, real_part, imag_part):
    return jnp.stack(
        [
            values[0] * real_part - values[1] * imag_part,
            values[0] * imag_part + values[1] * real_part,
        ]
    )


def contract(pattern, operand, matrix):
    return jnp.einsum(pattern, operand, matrix, preferred_element_type=jnp.float32)


def table_length(tables):
    return tables[0].shape[2] * tables[1].shape[2]


def forward_axis(values, tables, factor, patterns, trailing):
    outer_table, inner_table, twist_real, twist_imag = tables
    factor_real, factor_imag = factor
    if trailing:
        twist_real, twist_imag = (twist_real[..., None], twist_imag[..., None])
        factor_real, factor_imag = (factor_real[..., None], factor_imag[..., None])
    section_one = complex_times(
        contract(patterns[0], values, outer_table), twist_real, twist_imag
    ).astype(jnp.bfloat16)
    section_two = contract(patterns[1], section_one, inner_table)
    return complex_times(section_two, factor_real, factor_imag).astype(jnp.bfloat16)


def inverse_first(values, tables, patterns, trailing):
    outer_table, inner_table, twist_real, twist_imag = tables
    if trailing:
        twist_real, twist_imag = (twist_real[..., None], twist_imag[..., None])
    return complex_times(
        contract(patterns[2], values, inner_table), twist_real, -twist_imag
    ).astype(jnp.bfloat16)


def inverse_axis(values, tables, patterns, trailing):
    section_one = inverse_first(values, tables, patterns, trailing)
    return contract(patterns[3], section_one, tables[0]) * (1.0 / table_length(tables))


def window_matrix(half_width):
    positions = jnp.arange(XTILES, dtype=jnp.int32)
    difference = (positions[:, None] - positions[None, :]) % XTILES
    distance = jnp.minimum(difference, XTILES - difference)
    return (distance <= half_width).astype(jnp.float32)


def tile_statistics(first_moment, second_moment, half_width, tile_rows):
    window_mask = window_matrix(half_width)
    cells = ((2 * half_width + 1) * (TILE_X * tile_rows)).astype(jnp.float32)
    mean_one = jnp.dot(first_moment, window_mask, precision=lax.Precision.HIGHEST) / cells
    mean_two = jnp.dot(second_moment, window_mask, precision=lax.Precision.HIGHEST) / cells
    fluctuation = mean_two / (mean_one * mean_one + tiny_value) - 1.0
    return (fluctuation, mean_one * jnp.exp(-fluctuation))


def turn_pair(angle):
    quarter = jnp.round(angle * (2.0 / 3.141592653589793))
    rest = angle - quarter * 1.5703125
    rest = rest - quarter * 0.0004837512969970703
    rest = rest - quarter * 7.549789954891882e-08
    square = rest * rest
    sine = rest + rest * square * (
        -0.16666654611 + square * (0.0083321608736 + square * -0.00019515295891)
    )
    cosine = (
        1.0
        - 0.5 * square
        + square
        * square
        * (0.04166664568298827 + square * (-0.001388731625493765 + square * 2.443315711809948e-05))
    )
    turn = quarter.astype(jnp.int32) & 3
    swap = turn & 1 == 1
    sin_value = jnp.where(swap, cosine, sine)
    cos_value = jnp.where(swap, sine, cosine)
    sin_value = jnp.where(turn >= 2, -sin_value, sin_value)
    cos_value = jnp.where((turn == 1) | (turn == 2), -cos_value, cos_value)
    return (cos_value, sin_value)


def propagate_columns(phase_patch, tables_y, slant_factor, fresnel_y):
    patch_rows = phase_patch.shape[0]
    width_here = phase_patch.shape[1]
    outer_len = tables_y[0].shape[2]
    inner_len = tables_y[1].shape[2]
    turned_phase = slant_factor * phase_patch
    screen_field = jnp.stack(turn_pair(turned_phase)).astype(jnp.bfloat16)
    stacked = screen_field.reshape(2, outer_len, inner_len, width_here)
    spectral = forward_axis(stacked, tables_y, fresnel_y, column_patterns, True)
    result = inverse_axis(spectral, tables_y, column_patterns, True)
    return result.astype(jnp.bfloat16).reshape(2, patch_rows, width_here)


def body(white_noise, geometry, window, tile_map, link_gain, serving):
    row_count = lax.axis_size("row")
    tables = transform_tables(FIRST, SECOND)
    tables_y = transform_tables(row_count, ROWS_DEV)
    patch_len = row_count * ROWS_DEV
    rows_here = white_noise.shape[1]
    row_start = lax.axis_index(("dir", "row")) * rows_here
    row_ids = row_start + jnp.arange(rows_here, dtype=jnp.int32)
    column_ids = jnp.arange(N, dtype=jnp.int32)
    spectral_gain = spectral_filter(row_ids, column_ids)
    spectrum = (white_noise.astype(jnp.float32) * spectral_gain).astype(jnp.bfloat16)
    section_first = inverse_first(
        spectrum.reshape(2, rows_here, FIRST, SECOND), tables, row_patterns, False
    )
    half_screen = contract("zrkb,wzak->awrb", section_first, tables[0]) * (1.0 / N)
    half_screen = half_screen.astype(jnp.bfloat16)
    turned = lax.all_to_all(half_screen, "row", split_axis=0, concat_axis=0, tiled=True)
    slant_factor = 1.0 + 0.25 * geometry[0, 1].astype(jnp.float32)
    fresnel_x = fresnel_factor(geometry[0], FIRST, SECOND)
    fresnel_y = fresnel_factor(geometry[0], row_count, ROWS_DEV)
    offset_rows = N // 4 * geometry[0, 1]
    columns = SECOND
    blocks = row_count * rows_here // SECOND
    split = SECOND // rows_here
    block_start = lax.axis_index("dir") * blocks
    stacked = turned.reshape(blocks, split, 2, rows_here, columns)
    inner_split = tables[1].reshape(2, 2, SECOND, split, rows_here)
    twist_real = lax.dynamic_slice_in_dim(tables[2], block_start, blocks, 0)[..., None]
    twist_imag = lax.dynamic_slice_in_dim(tables[3], block_start, blocks, 0)[..., None]
    section_one = complex_times(
        contract("khzrx,wzbhr->wkbx", stacked, inner_split), twist_real, -twist_imag
    )
    section_one = section_one.astype(jnp.bfloat16)
    outer_count = patch_len // SECOND
    outer_ids = (offset_rows // SECOND + jnp.arange(outer_count, dtype=jnp.int32)) % FIRST
    patch_outer = jnp.take(tables[0][0], outer_ids, axis=1)
    gathered = lax.all_gather(section_one, "dir", axis=1, tiled=True)
    depth = gathered.shape[0] * gathered.shape[1]
    patch_matrix = jnp.transpose(patch_outer, (1, 0, 2)).reshape(outer_count, depth)
    phase_patch = jnp.dot(
        patch_matrix, gathered.reshape(depth, -1), preferred_element_type=jnp.float32
    )
    phase_patch = phase_patch.reshape(patch_len, columns) * (1.0 / N)
    screen_field = propagate_columns(phase_patch, tables_y, slant_factor, fresnel_y)
    stacked_field = screen_field.reshape(2, row_count, ROWS_DEV, columns)
    portion = lax.all_to_all(stacked_field, "row", split_axis=1, concat_axis=3, tiled=True)
    item_count = portion.shape[2]
    stacked = portion.reshape(2, item_count, FIRST, SECOND)
    spectral = forward_axis(stacked, tables, fresnel_x, row_patterns, False)
    wave_field = inverse_axis(spectral, tables, row_patterns, False)
    intensity = wave_field[0] * wave_field[0] + wave_field[1] * wave_field[1]
    intensity = intensity.reshape(item_count, XTILES, TILE_X)
    tile_one = jnp.sum(intensity, axis=2)
    tile_two = jnp.sum(intensity * intensity, axis=2)
    tile_rows = ROWS_DEV // YTILES
    first_moment = jnp.sum(tile_one.reshape(YTILES, tile_rows, XTILES), axis=1)
    second_moment = jnp.sum(tile_two.reshape(YTILES, tile_rows, XTILES), axis=1)
    fluctuation, faded_power = tile_statistics(first_moment, second_moment, window[0], tile_rows)
    tile_total = faded_power.shape[0] * faded_power.shape[1]
    local_tile = tile_map[0] - lax.axis_index("row") * tile_total
    inside = (local_tile >= 0) & (local_tile < tile_total)
    tile_row = local_tile // XTILES
    tile_column = local_tile % XTILES
    pick_row = (tile_row[:, None] == jnp.arange(YTILES, dtype=jnp.int32)[None, :]).astype(
        jnp.float32
    )
    row_values = jnp.dot(pick_row, faded_power, precision=lax.Precision.HIGHEST)
    pick_column = tile_column[:, None] == jnp.arange(XTILES, dtype=jnp.int32)[None, :]
    looked = jnp.sum(jnp.where(pick_column, row_values, 0.0), axis=1)
    looked = jnp.where(inside, looked, 0.0)
    received = link_gain[0] * looked
    direction = lax.axis_index("dir")
    serves_here = serving == direction
    signal_part = jnp.where(serves_here, received, 0.0)
    interference_part = jnp.where(serves_here, 0.0, received)
    dir_count = lax.axis_size("dir")
    share_size = serving.shape[0] // (dir_count * row_count)
    parts = jnp.stack([signal_part, interference_part]).reshape(2, dir_count, row_count, share_size)
    parts = lax.all_to_all(parts, "row", split_axis=2, concat_axis=2, tiled=True)
    parts = jnp.sum(parts, axis=2, keepdims=True)
    parts = lax.all_to_all(parts, "dir", split_axis=1, concat_axis=1, tiled=True)
    parts = jnp.sum(parts, axis=(1, 2))
    signal, interference = (parts[0], parts[1])
    signal_ratio = jnp.log10(signal / (interference + noise_floor))
    return (fluctuation[None], signal_ratio)


def solution(mesh):
    return jax.shard_map(
        body,
        mesh=mesh,
        in_specs=(
            P(None, ("dir", "row"), None),
            P("dir", None),
            P("dir"),
            P("dir", None),
            P("dir", None),
            P(),
        ),
        out_specs=(P("dir", "row", None), P(("dir", "row"))),
        check_vma=False,
    )
```

profile of v0, /device:TPU:1, one launch (start us, length us, event | category | flops | bytes accessed | tf_op | source)
XLA Modules:
  0.0 306.3 jit_solution(62604927626251971)
XLA Ops:
  8.5 1.1 multiply_convert_fusion
  10.7 1.1 copy.128
  11.8 22.2 %all-to-all-start = ((bf16[64,2,16,128]{3,2,1,0:T(8,128)(2,1)}), bf16[64,2,16,128]{3,2,1,0:T(8,128)(2,1)S(1)}, u32[]{:S(2)}, u32[]{:S(2)}) async-start(bf16[64,2,16,128]{3,2,1,0:T(8,128)(2,1)} %copy.128), calls=%async_computation | async-start | bytes 1048576 | tf_op jit(solution)/shard_map/all_to_all | solution.py:199
  34.8 21.1 %all-to-all-done = bf16[64,2,16,128]{3,2,1,0:T(8,128)(2,1)S(1)} async-done(((bf16[64,2,16,128]{3,2,1,0:T(8,128)(2,1)}), bf16[64,2,16,128]{3,2,1,0:T(8,128)(2,1)S(1)}, u32[]{:S(2)}, u32[]{:S(2)}) %all-to-all-start) | async-done | bytes 524320 | tf_op jit(solution)/shard_map/all_to_all | solution.py:199
  56.6 0.8 pad_maximum_fusion.7
  57.5 0.6 fusion.173
  59.4 0.6 gather_fusion
  61.6 105.1 %all-gather.2.cloned.1.call-done = bf16[2,64,128,128]{3,2,1,0:T(8,128)(2,1)} async-done(((bf16[2,8,128,128]{3,2,1,0:T(8,128)(2,1)}), bf16[2,64,128,128]{3,2,1,0:T(8,128)(2,1)}) %all-gather.2.cloned.1.call-update) | async-done | bytes 4194320 | tf_op jit(solution)/shard_map/all_gather | solution.py:219
  166.7 4.5 %convolution_multiply_fusion = f32[16,16384]{1,0:T(8,128)S(1)} fusion(bf16[16,128]{1,0:T(8,128)(2,1)S(1)} %reshape.886, bf16[16,8,128,128]{3,2,1,0:T(8,128)(2,1)} %bitcast.201, f32[]{:T(128)} %bitcast.39), kind=kOutput, calls=%fused_computation.1 | convolution fusion | flops 67371008 | bytes 5246980 | tf_op jit(solution)/shard_map/dot_general | solution.py:222
  171.4 1.6 fusion.18
  173.0 0.5 convolution_bitcast_fusion.5
  173.4 0.7 subtract_convert_fusion.5
  174.3 0.9 convolution_bitcast_fusion.4
  175.2 0.7 subtract_convert_fusion.4
  175.9 0.5 convolution_bitcast_fusion.3
  176.3 1.2 copy.255
  177.5 0.7 subtract_convert_fusion.3
  178.3 0.5 fusion.3
  178.8 1.7 copy.139
  180.4 11.7 %all-to-all-start.1 = ((bf16[2,64,32,128]{3,2,0,1:T(8,128)(2,1)}), bf16[2,64,32,128]{3,2,0,1:T(8,128)(2,1)S(1)}, u32[]{:S(2)}, u32[]{:S(2)}) async-start(bf16[2,64,32,128]{3,2,0,1:T(8,128)(2,1)} %copy.139), calls=%async_computation.1 | async-start | bytes 2097152 | tf_op jit(solution)/shard_map/all_to_all | solution.py:228
  193.1 53.6 %all-to-all-done.1 = bf16[2,64,32,128]{3,2,0,1:T(8,128)(2,1)S(1)} async-done(((bf16[2,64,32,128]{3,2,0,1:T(8,128)(2,1)}), bf16[2,64,32,128]{3,2,0,1:T(8,128)(2,1)S(1)}, u32[]{:S(2)}, u32[]{:S(2)}) %all-to-all-start.1) | async-done | bytes 1048608 | tf_op jit(solution)/shard_map/all_to_all | solution.py:228
  246.6 0.9 convolution_bitcast_fusion.2
  247.8 0.4 convolution_bitcast_fusion.1
  248.6 0.5 convolution_bitcast_fusion
  249.4 0.5 fusion.2
  250.4 1.1 fusion.172
  252.0 2.3 fusion.4
  255.2 19.7 %all_to_all.30 = f32[64,1,256]{2,1,0:T(1,128)S(1)} all-to-all(f32[64,1,256]{2,1,0:T(1,128)S(1)} %reshape.1063), channel_id=1, replica_groups=mesh['dir'=8,'row'=64] {'row'}, dimensions={0} | all-to-all | bytes 131072 | tf_op jit(solution)/shard_map/all_to_all | solution.py:261
  274.9 0.5 broadcast.1677
  275.4 0.8 reduce
  276.5 22.5 %all_to_all.31 = f32[2,8,1,16]{3,0,2,1:T(2,128)S(1)} all-to-all(f32[2,8,1,16]{3,0,2,1:T(2,128)S(1)} %copy.149), channel_id=1, replica_groups=mesh['dir'=8,'row'=64] {'dir'}, dimensions={1} | all-to-all | bytes 2048 | tf_op jit(solution)/shard_map/all_to_all | solution.py:263
  299.0 0.5 multiply_bitcast_fusion
  (72 shorter events, 8.1 us)
Async XLA Ops:
  11.8 44.1 %all-to-all-start = ((bf16[64,2,16,128]{3,2,1,0:T(8,128)(2,1)}), bf16[64,2,16,128]{3,2,1,0:T(8,128)(2,1)S(1)}, u32[]{:S(2)}, u32[]{:S(2)}) async-start(bf16[64,2,16,128]{3,2,1,0:T(8,128)(2,1)} %copy.128), calls=%async_computation | async-start | bytes 1048576 | tf_op jit(solution)/shard_map/all_to_all | solution.py:199
  34.1 132.6 %all-gather.2.cloned.1.call-start = ((), (), s32[]{:S(2)}) async-start(), calls=%async_computation.4 | async-start | bytes 4718592 | tf_op jit(solution)/shard_map/all_gather | solution.py:219
  55.9 1.5 copy-start.3
  178.7 14.2 %copy-start.1 = (s32[1,8192]{1,0:T(1,128)S(1)}, s32[1,8192]{1,0:T(1,128)}, u32[]{:S(2)}) copy-start(s32[1,8192]{1,0:T(1,128)} %param.9) | copy-start | bytes 98308
  180.4 66.2 %all-to-all-start.1 = ((bf16[2,64,32,128]{3,2,0,1:T(8,128)(2,1)}), bf16[2,64,32,128]{3,2,0,1:T(8,128)(2,1)S(1)}, u32[]{:S(2)}, u32[]{:S(2)}) async-start(bf16[2,64,32,128]{3,2,0,1:T(8,128)(2,1)} %copy.139), calls=%async_computation.1 | async-start | bytes 2097152 | tf_op jit(solution)/shard_map/all_to_all | solution.py:228
  251.8 2.5 copy-start
  251.8 2.5 copy-start.2
  252.0 2.3 copy-start.4
Sparse Core Ops, SparseCore 0:
  57.6 109.0 all-gather.1
where the time goes:
time: 307 us; the launch traced here: 306 us
  waiting for transfers between devices  180 us (59%)
  blocking collectives  42.1 us (14%)
  starting transfers between devices  34.2 us (11%)
  between operations  17.2 us (6%)
  other arithmetic  12.8 us (4%)
  matrix products  12.6 us (4%)
  local copies, waits for them, and re-layouts  7.6 us (2%)
    all_gather x1, waiting for transfers between devices, body(): gathered = lax.all_gather(section_one, 'dir', axis=1, tiled=True)  105 us
    all_to_all x1, waiting for transfers between devices, body(): lax.all_to_all(stacked_field, 'row', split_axis=1, concat_axis=3, tiled=T...  53.6 us
    all_to_all x1, blocking collectives, body(): lax.all_to_all(parts, 'dir', split_axis=1, concat_axis=1, tiled=True)  22.5 us
    all_to_all x1, starting transfers between devices, body(): lax.all_to_all(half_screen, 'row', split_axis=0, concat_axis=0, tiled=True)  22.2 us
    all_to_all x1, waiting for transfers between devices, body(): lax.all_to_all(half_screen, 'row', split_axis=0, concat_axis=0, tiled=True)  21.1 us
    all_to_all x1, blocking collectives, body(): lax.all_to_all(parts, 'row', split_axis=2, concat_axis=2, tiled=True)  19.7 us
    all_to_all x1, starting transfers between devices, body(): lax.all_to_all(stacked_field, 'row', split_axis=1, concat_axis=3, tiled=T...  11.7 us
    another operation x16, other arithmetic  6.5 us
  transfers between devices with their start and end apart: 3, of which 3 were waited for; matrix products, arithmetic and copies ran while one was open for 1% of the time, Pallas kernels for 0%

commit v1 on v0

--- a/solution.py
+++ b/solution.py
@@ -216,7 +216,9 @@
     outer_count = patch_len // SECOND
     outer_ids = (offset_rows // SECOND + jnp.arange(outer_count, dtype=jnp.int32)) % FIRST
     patch_outer = jnp.take(tables[0][0], outer_ids, axis=1)
-    gathered = lax.all_gather(section_one, "dir", axis=1, tiled=True)
+    gathered = jnp.concatenate(
+        lax.all_to_all(jnp.stack([section_one] * lax.axis_size("dir")), "dir", 0, 0), axis=1
+    )
     depth = gathered.shape[0] * gathered.shape[1]
     patch_matrix = jnp.transpose(patch_outer, (1, 0, 2)).reshape(outer_count, depth)
     phase_patch = jnp.dot(

time: 307 us -> 381 us (1.24)
  waiting for transfers between devices: 180 us -> 245 us
  starting transfers between devices: 34.2 us -> 48.8 us
  between operations: 17.2 us -> 3.8 us
  local copies, waits for them, and re-layouts: 7.6 us -> 13.1 us
  blocking collectives: 42.1 us -> 47.4 us
    all_to_all x0 -> x1, waiting for transfers between devices: none -> 181 us  [body(): lax.all_to_all(jnp.stack([section_one] * lax.axis_size('dir')), 'dir', 0, 0)]
    all_gather x1 -> x0, waiting for transfers between devices: 105 us -> none  [body(): gathered = lax.all_gather(section_one, 'dir', axis=1, tiled=True)]
    all_to_all x0 -> x1, starting transfers between devices: none -> 20.9 us  [body(): lax.all_to_all(jnp.stack([section_one] * lax.axis_size('dir')), 'dir', 0, 0)]
    all_to_all x1, blocking collectives: 19.7 us -> 30.9 us  [body(): lax.all_to_all(parts, 'row', split_axis=2, concat_axis=2, tiled=True)]
    all_to_all x1, waiting for transfers between devices: 53.6 us -> 42.6 us  [body(): lax.all_to_all(stacked_field, 'row', split_axis=1, concat_axis=3, tiled=T...]
    all_to_all x1, starting transfers between devices: 11.7 us -> 5.7 us  [body(): lax.all_to_all(stacked_field, 'row', split_axis=1, concat_axis=3, tiled=T...]
    all_to_all x1, blocking collectives: 22.5 us -> 16.5 us  [body(): lax.all_to_all(parts, 'dir', split_axis=1, concat_axis=1, tiled=True)]
where the time goes in v1:
time: 381 us
  waiting for transfers between devices  245 us (64%)
  starting transfers between devices  48.8 us (13%)
  blocking collectives  47.4 us (12%)
  local copies, waits for them, and re-layouts  13.1 us (3%)
  other arithmetic  12 us (3%)
  matrix products  10.5 us (3%)
    all_to_all x1, waiting for transfers between devices, body(): lax.all_to_all(jnp.stack([section_one] * lax.axis_size('dir')), 'dir', 0, 0)  181 us
    all_to_all x1, waiting for transfers between devices, body(): lax.all_to_all(stacked_field, 'row', split_axis=1, concat_axis=3, tiled=T...  42.6 us
    all_to_all x1, blocking collectives, body(): lax.all_to_all(parts, 'row', split_axis=2, concat_axis=2, tiled=True)  30.9 us
    all_to_all x1, starting transfers between devices, body(): lax.all_to_all(half_screen, 'row', split_axis=0, concat_axis=0, tiled=True)  22.2 us
    all_to_all x1, waiting for transfers between devices, body(): lax.all_to_all(half_screen, 'row', split_axis=0, concat_axis=0, tiled=True)  21.3 us
    all_to_all x1, starting transfers between devices, body(): lax.all_to_all(jnp.stack([section_one] * lax.axis_size('dir')), 'dir', 0, 0)  20.9 us
    all_to_all x1, blocking collectives, body(): lax.all_to_all(parts, 'dir', split_axis=1, concat_axis=1, tiled=True)  16.5 us
  transfers between devices with their start and end apart: 3, of which 3 were waited for; matrix products, arithmetic and copies ran while one was open for 1% of the time, Pallas kernels for 0%

profile of v1, /device:TPU:1, one launch (start us, length us, event | category | flops | bytes accessed | tf_op | source)
XLA Modules:
  0.0 380.9 jit_solution(10352149233500588817)
XLA Ops:
  2.0 1.1 multiply_convert_fusion
  4.1 1.1 copy.131
  5.3 22.2 %all-to-all-start = ((bf16[64,2,16,128]{3,2,1,0:T(8,128)(2,1)}), bf16[64,2,16,128]{3,2,1,0:T(8,128)(2,1)S(1)}, u32[]{:S(2)}, u32[]{:S(2)}) async-start(bf16[64,2,16,128]{3,2,1,0:T(8,128)(2,1)} %copy.131), calls=%async_computation | async-start | bytes 1048576 | tf_op jit(solution)/shard_map/all_to_all | solution.py:199
  28.0 21.3 %all-to-all-done = bf16[64,2,16,128]{3,2,1,0:T(8,128)(2,1)S(1)} async-done(((bf16[64,2,16,128]{3,2,1,0:T(8,128)(2,1)}), bf16[64,2,16,128]{3,2,1,0:T(8,128)(2,1)S(1)}, u32[]{:S(2)}, u32[]{:S(2)}) %all-to-all-start) | async-done | bytes 524320 | tf_op jit(solution)/shard_map/all_to_all | solution.py:199
  50.1 3.0 stack.179
  53.1 20.9 %all-to-all-start.1 = ((bf16[8,2,8,128,128]{4,3,2,1,0:T(8,128)(2,1)}), bf16[8,2,8,128,128]{4,3,2,1,0:T(8,128)(2,1)}, u32[]{:S(2)}, u32[]{:S(2)}) async-start(bf16[8,2,8,128,128]{4,3,2,1,0:T(8,128)(2,1)} %stack.179), calls=%async_computation.1 | async-start | bytes 8388608 | tf_op jit(solution)/shard_map/all_to_all | solution.py:220
  74.0 0.6 fusion.173
  76.0 0.6 gather_fusion
  78.1 181.4 %all-to-all-done.1 = bf16[8,2,8,128,128]{4,3,2,1,0:T(8,128)(2,1)} async-done(((bf16[8,2,8,128,128]{4,3,2,1,0:T(8,128)(2,1)}), bf16[8,2,8,128,128]{4,3,2,1,0:T(8,128)(2,1)}, u32[]{:S(2)}, u32[]{:S(2)}) %all-to-all-start.1) | async-done | bytes 4194336 | tf_op jit(solution)/shard_map/all_to_all | solution.py:220
  259.5 2.5 copy.132
  262.0 2.3 convolution_multiply_fusion
  264.5 1.6 fusion.18
  266.6 0.7 subtract_convert_fusion.5
  267.4 0.9 convolution_bitcast_fusion.4
  268.3 0.7 subtract_convert_fusion.4
  269.0 0.5 convolution_bitcast_fusion.3
  269.5 1.2 copy.259
  270.7 0.7 subtract_convert_fusion.3
  271.4 0.5 fusion.3
  271.9 1.6 copy.143
  273.5 5.7 %all-to-all-start.2 = ((bf16[2,64,32,128]{3,2,0,1:T(8,128)(2,1)}), bf16[2,64,32,128]{3,2,0,1:T(8,128)(2,1)S(1)}, u32[]{:S(2)}, u32[]{:S(2)}) async-start(bf16[2,64,32,128]{3,2,0,1:T(8,128)(2,1)} %copy.143), calls=%async_computation.2 | async-start | bytes 2097152 | tf_op jit(solution)/shard_map/all_to_all | solution.py:230
  280.2 42.6 %all-to-all-done.2 = bf16[2,64,32,128]{3,2,0,1:T(8,128)(2,1)S(1)} async-done(((bf16[2,64,32,128]{3,2,0,1:T(8,128)(2,1)}), bf16[2,64,32,128]{3,2,0,1:T(8,128)(2,1)S(1)}, u32[]{:S(2)}, u32[]{:S(2)}) %all-to-all-start.2) | async-done | bytes 1048608 | tf_op jit(solution)/shard_map/all_to_all | solution.py:230
  322.8 0.9 convolution_bitcast_fusion.2
  324.7 0.5 convolution_bitcast_fusion
  325.5 0.5 fusion.2
  326.6 1.1 fusion.172
  328.1 2.3 fusion.4
  331.3 30.9 %all_to_all.35 = f32[64,1,256]{2,1,0:T(1,128)S(1)} all-to-all(f32[64,1,256]{2,1,0:T(1,128)S(1)} %reshape.1070), channel_id=1, replica_groups=mesh['dir'=8,'row'=64] {'row'}, dimensions={0} | all-to-all | bytes 131072 | tf_op jit(solution)/shard_map/all_to_all | solution.py:263
  362.3 0.5 broadcast.1678
  362.8 0.8 reduce
  363.9 16.5 %all_to_all.36 = f32[2,8,1,16]{3,0,2,1:T(2,128)S(1)} all-to-all(f32[2,8,1,16]{3,0,2,1:T(2,128)S(1)} %copy.153), channel_id=1, replica_groups=mesh['dir'=8,'row'=64] {'dir'}, dimensions={1} | all-to-all | bytes 2048 | tf_op jit(solution)/shard_map/all_to_all | solution.py:265
  380.4 0.5 multiply_bitcast_fusion
  (73 shorter events, 8.8 us)
Async XLA Ops:
  5.3 44.1 %all-to-all-start = ((bf16[64,2,16,128]{3,2,1,0:T(8,128)(2,1)}), bf16[64,2,16,128]{3,2,1,0:T(8,128)(2,1)S(1)}, u32[]{:S(2)}, u32[]{:S(2)}) async-start(bf16[64,2,16,128]{3,2,1,0:T(8,128)(2,1)} %copy.131), calls=%async_computation | async-start | bytes 1048576 | tf_op jit(solution)/shard_map/all_to_all | solution.py:199
  53.1 20.9 %copy-start.3 = (s32[1,2]{1,0:T(1,128)S(1)}, s32[1,2]{1,0:T(1,128)}, u32[]{:S(2)}) copy-start(s32[1,2]{1,0:T(1,128)} %param.7) | copy-start | bytes 28
  53.1 206.4 %all-to-all-start.1 = ((bf16[8,2,8,128,128]{4,3,2,1,0:T(8,128)(2,1)}), bf16[8,2,8,128,128]{4,3,2,1,0:T(8,128)(2,1)}, u32[]{:S(2)}, u32[]{:S(2)}) async-start(bf16[8,2,8,128,128]{4,3,2,1,0:T(8,128)(2,1)} %stack.179), calls=%async_computation.1 | async-start | bytes 8388608 | tf_op jit(solution)/shard_map/all_to_all | solution.py:220
  271.9 8.2 %copy-start.1 = (s32[1,8192]{1,0:T(1,128)S(1)}, s32[1,8192]{1,0:T(1,128)}, u32[]{:S(2)}) copy-start(s32[1,8192]{1,0:T(1,128)} %param.9) | copy-start | bytes 98308
  273.5 49.3 %all-to-all-start.2 = ((bf16[2,64,32,128]{3,2,0,1:T(8,128)(2,1)}), bf16[2,64,32,128]{3,2,0,1:T(8,128)(2,1)S(1)}, u32[]{:S(2)}, u32[]{:S(2)}) async-start(bf16[2,64,32,128]{3,2,0,1:T(8,128)(2,1)} %copy.143), calls=%async_computation.2 | async-start | bytes 2097152 | tf_op jit(solution)/shard_map/all_to_all | solution.py:230
  327.9 2.5 copy-start
  328.0 2.5 copy-start.2
  328.1 2.3 copy-start.4
